TPU v7x, 128 devices: a whole 4x4x4 slice. The times are simulated.
128 devices in a mesh: seq: 16 (over x_hi, z, core), tp: 8 (over y, x_lo).
Axes of the slice: x: 4 (x_hi: 2, x_lo: 2; x = x_hi * 2 + x_lo), y: 4, z: 4, core: 2. Of those that a mesh axis runs over, the one named last changes fastest.
Arguments:
- tokens: bfloat16 [4, 2048, 4096], P(None, 'seq', 'tp'), may hold values from -6 to 6
- new_tokens: bfloat16 [4, 4096], P(None, 'tp'), may hold values from -6 to 6
- w_qkv: bfloat16 [3, 4096, 4096], P(None, None, 'tp')
- w_out: bfloat16 [4096, 4096], P('tp')
- q_gain: float32 [4096], P('tp'), may hold values from 0.5 to 6
- k_gain: float32 [4096], P('tp'), may hold values from 0.5 to 6
- post_gain: float32 [4096], P('tp'), may hold values from 0.5 to 1.5
- lengths: int32 [4], replicated, may hold values from 1 to 2048, 6144 in all
Outputs:
- hidden_out: bfloat16 [4, 2048, 4096], P(None, 'seq', 'tp')
- new_out: bfloat16 [4, 4096], P(None, 'tp')
Inputs may be any that keep to these rules, and one draw needn't show every extreme that they name: `lengths`: one prompt has exactly 2048 live tokens.
All inputs are finite; a program needn't handle non-finite values.
Results may differ from a plain program's by a relative error of at most 0.012.
The roundings to bfloat16 on the way count: a program that leaves them out, or rounds other values in their place, can miss the bound.
Values may be sent and summed in bfloat16 or wider, within the bound.
No kernel may reach another device: no remote copies, remote signals or barrier semaphores. Data moves between devices by JAX's collectives and lax.ppermute only.
A program may use at most 128 MiB of HBM per device.

v0:
```python
from functools import partial
import jax
import jax.numpy as jnp
from jax import lax
from jax.sharding import PartitionSpec as P

HD = 128
rope_base = 500000.0
norm_eps = 1e-06
masked_fill = -1e30


def joined(value, axis, combine):
    everything = jax.tree.map(lambda part: lax.all_gather(part, axis), value)
    initial = jax.tree.map(lambda part: part[0], everything)

    def hop(k, so_far):
        return combine(so_far, jax.tree.map(lambda part: part[k], everything))

    return lax.fori_loop(1, lax.axis_size(axis), hop, initial)


def rotate(values, position):
    half = values.shape[-1] // 2
    freq = rope_base ** (-(jnp.arange(half, dtype=jnp.float32) * 2.0) / values.shape[-1])
    angle = position.astype(jnp.float32)[..., None] * freq
    cosine = jnp.cos(angle)
    sine = jnp.sin(angle)
    lower = values[..., :half]
    upper = values[..., half:]
    return jnp.concatenate([lower * cosine - upper * sine, upper * cosine + lower * sine], -1)


def fold_step(carry, pieces, start, queries, query_pos, lengths, scale):
    running_max, running_sum, running_acc = carry
    key_piece, value_piece = pieces
    count = key_piece.shape[1]
    scores = (
        jnp.einsum("sphe,snhe->shpn", queries, key_piece, preferred_element_type=jnp.float32)
        * scale
    )
    key_pos = jnp.arange(count, dtype=jnp.int32)
    valid = (key_pos[None, None, :] <= query_pos[None, :, None]) & (
        key_pos[None, None, :] < lengths[:, None, None]
    )
    valid = valid[:, None, :, :]
    scores = jnp.where(valid, scores, masked_fill)
    new_max = jnp.maximum(running_max, jnp.max(scores, -1))
    weights = jnp.where(valid, jnp.exp(scores - new_max[..., None]), 0.0)
    running_sum = jnp.sum(weights, -1)
    running_acc = jnp.einsum(
        "shpn,snhe->shpe",
        weights.astype(jnp.bfloat16),
        value_piece,
        preferred_element_type=jnp.float32,
    )
    return (new_max, running_sum, running_acc)


def combine(first, second):
    first_max, first_sum, first_acc = first
    second_max, second_sum, second_acc = second
    top = jnp.maximum(first_max, second_max)
    first_factor = jnp.exp(first_max - top)
    second_factor = jnp.exp(second_max - top)
    return (
        top,
        first_sum * first_factor + second_sum * second_factor,
        first_acc * first_factor[..., None] + second_acc * second_factor[..., None],
    )


def body(tokens, new_tokens, w_qkv, w_out, q_gain, k_gain, post_gain, lengths):
    seqs, pos_dev, width_local = tokens.shape
    heads_local = width_local // HD
    full_width = w_qkv.shape[1]
    prompt_rows = seqs * pos_dev
    flat_rows = tokens.reshape(prompt_rows, width_local)
    row_piece = lax.all_gather(flat_rows, "tp", axis=1, tiled=True)
    new_piece = lax.all_gather(new_tokens, "tp", axis=1, tiled=True)
    proj_rows = jnp.einsum("tn,cnf->ctf", row_piece, w_qkv, preferred_element_type=jnp.float32)
    proj_new = jnp.einsum("tn,cnf->ctf", new_piece, w_qkv, preferred_element_type=jnp.float32)
    query_rows, key_rows = (proj_rows[0], proj_rows[1])
    query_fresh, key_fresh = (proj_new[0], proj_new[1])
    query_sq, key_sq, query_new_sq, key_new_sq = lax.psum(
        (
            jnp.sum(query_rows * query_rows, -1),
            jnp.sum(key_rows * key_rows, -1),
            jnp.sum(query_fresh * query_fresh, -1),
            jnp.sum(key_fresh * key_fresh, -1),
        ),
        "tp",
    )

    def normed(values, square_sum, gain):
        return values * lax.rsqrt(square_sum[:, None] / full_width + norm_eps) * gain

    seq_index = lax.axis_index("seq")
    query_pos = seq_index * pos_dev + jnp.arange(pos_dev, dtype=jnp.int32)
    row_pos = jnp.tile(query_pos, seqs)
    queries = rotate(
        normed(query_rows, query_sq, q_gain).reshape(prompt_rows, heads_local, HD), row_pos[:, None]
    )
    queries = queries.astype(jnp.bfloat16).reshape(seqs, pos_dev, heads_local, HD)
    keys = rotate(
        normed(key_rows, key_sq, k_gain).reshape(prompt_rows, heads_local, HD), row_pos[:, None]
    )
    keys = keys.astype(jnp.bfloat16).reshape(seqs, pos_dev, heads_local, HD)
    values = proj_rows[2].astype(jnp.bfloat16).reshape(seqs, pos_dev, heads_local, HD)
    new_queries = rotate(
        normed(query_fresh, query_new_sq, q_gain).reshape(seqs, heads_local, HD), lengths[:, None]
    ).astype(jnp.bfloat16)
    new_keys = rotate(
        normed(key_fresh, key_new_sq, k_gain).reshape(seqs, heads_local, HD), lengths[:, None]
    ).astype(jnp.bfloat16)
    new_values = proj_new[2].astype(jnp.bfloat16).reshape(seqs, heads_local, HD)
    scale = HD ** (-0.5)
    start_carry = (
        jnp.full((seqs, heads_local, pos_dev), masked_fill, jnp.float32),
        jnp.zeros((seqs, heads_local, pos_dev), jnp.float32),
        jnp.zeros((seqs, heads_local, pos_dev, HD), jnp.float32),
    )
    stepper = partial(fold_step, queries=queries, query_pos=query_pos, lengths=lengths, scale=scale)
    final_max, final_sum, final_acc = stepper(
        start_carry,
        (
            lax.all_gather(keys, "seq", axis=1, tiled=True),
            lax.all_gather(values, "seq", axis=1, tiled=True),
        ),
        jnp.int32(0),
    )
    attention = (
        (final_acc / final_sum[..., None])
        .transpose(0, 2, 1, 3)
        .reshape(prompt_rows, width_local)
        .astype(jnp.bfloat16)
    )
    local_scores = (
        jnp.einsum("she,sphe->shp", new_queries, keys, preferred_element_type=jnp.float32) * scale
    )
    live = (query_pos[None, :] < lengths[:, None])[:, None, :]
    local_scores = jnp.where(live, local_scores, masked_fill)
    local_max = jnp.max(local_scores, -1)
    local_weights = jnp.where(live, jnp.exp(local_scores - local_max[..., None]), 0.0)
    local_sum = jnp.sum(local_weights, -1)
    local_acc = jnp.einsum(
        "shp,sphe->she",
        local_weights.astype(jnp.bfloat16),
        values,
        preferred_element_type=jnp.float32,
    )
    merged_max, merged_sum, merged_acc = joined((local_max, local_sum, local_acc), "seq", combine)
    self_score = (
        jnp.einsum("she,she->sh", new_queries, new_keys, preferred_element_type=jnp.float32) * scale
    )
    new_top = jnp.maximum(merged_max, self_score)
    keep_factor = jnp.exp(merged_max - new_top)
    own_weight = jnp.exp(self_score - new_top)
    new_total = merged_sum * keep_factor + own_weight
    own_rounded = lax.optimization_barrier(own_weight.astype(jnp.bfloat16)).astype(jnp.float32)
    numer = merged_acc * keep_factor[..., None] + own_rounded[..., None] * new_values.astype(
        jnp.float32
    )
    new_attention = (numer / new_total[..., None]).reshape(seqs, width_local).astype(jnp.bfloat16)
    part_rows = jnp.dot(attention, w_out, preferred_element_type=jnp.float32)
    part_new = jnp.dot(new_attention, w_out, preferred_element_type=jnp.float32)
    sum_rows, sum_new = (
        lax.psum(part_rows.astype(jnp.bfloat16), "tp").astype(jnp.float32),
        lax.psum(part_new.astype(jnp.bfloat16), "tp").astype(jnp.float32),
    )
    mean_rows = jnp.mean(sum_rows * sum_rows, -1)
    mean_new = jnp.mean(sum_new * sum_new, -1)
    offset = lax.axis_index("tp") * width_local
    own_rows = lax.dynamic_slice_in_dim(sum_rows, offset, width_local, 1)
    own_new = lax.dynamic_slice_in_dim(sum_new, offset, width_local, 1)
    out_rows = (
        flat_rows.astype(jnp.float32)
        + own_rows * lax.rsqrt(mean_rows[:, None] + norm_eps) * post_gain
    )
    out_new = (
        new_tokens.astype(jnp.float32)
        + own_new * lax.rsqrt(mean_new[:, None] + norm_eps) * post_gain
    )
    return (
        out_rows.astype(jnp.bfloat16).reshape(seqs, pos_dev, width_local),
        out_new.astype(jnp.bfloat16),
    )


def solution(mesh):
    in_specs = (
        P(None, "seq", "tp"),
        P(None, "tp"),
        P(None, None, "tp"),
        P("tp", None),
        P("tp"),
        P("tp"),
        P("tp"),
        P(),
    )
    out_specs = (P(None, "seq", "tp"), P(None, "tp"))
    return jax.shard_map(body, mesh=mesh, in_specs=in_specs, out_specs=out_specs, check_vma=False)
```

profile of v0, /device:TPU:1, one launch (start us, length us, event | category | flops | bytes accessed | tf_op | source)
XLA Modules:
  0.0 495.8 jit_solution(5832578119530907273)
XLA Ops:
  7.2 0.7 all-gather.9.cloned.1.call-update
  7.9 23.3 %all_gather.33 = bf16[4,4096]{1,0:T(4,128)(2,1)S(1)} all-gather(bf16[4,512]{1,0:T(4,128)(2,1)} %param.11), channel_id=1, replica_groups=mesh['seq'=16,'tp'=8] {'tp'}, dimensions={1}, use_global_device_ids=true | all-gather | bytes 36864 | tf_op jit(solution)/shard_map/all_gather | solution.py:80
  31.3 6.3 %convolution_bitcast_fusion = f32[3,4,512]{2,1,0:T(4,128)S(1)} fusion(bf16[3,4096,512]{2,1,0:T(8,128)(2,1)} %param.12, bf16[4,4096]{1,0:T(4,128)(2,1)S(1)} %all_gather.33), kind=kOutput, calls=%fused_computation.23 | convolution fusion | flops 50331648 | bytes 12640256 | tf_op jit(solution)/shard_map/tn,cnf->ctf/dot_general | solution.py:82
  37.8 0.5 multiply_cosine_fusion
  38.4 65.3 %all-gather.9.cloned.1.call-done = bf16[512,4096]{1,0:T(8,128)(2,1)} async-done(((bf16[512,512]{1,0:T(8,128)(2,1)}), bf16[512,4096]{1,0:T(8,128)(2,1)}) %all-gather.9.cloned.1.call-update) | async-done | bytes 4194320 | tf_op jit(solution)/shard_map/all_gather | solution.py:79
  103.7 10.6 %fusion.11 = f32[3,512,512]{1,2,0:T(8,128)S(1)} fusion(bf16[3,4096,512]{2,1,0:T(8,128)(2,1)} %param.12, bf16[512,4096]{1,0:T(8,128)(2,1)} %all-gather.9.cloned.1.call-done), kind=kOutput, calls=%fused_computation.21 | convolution fusion | flops 6442450944 | bytes 19922944 | tf_op jit(solution)/shard_map/tn,cnf->ctf/dot_general | solution.py:81
  114.3 1.7 copy-done.1
  116.0 0.4 multiply_reduce_fusion.2
  116.4 14.3 %all-reduce = (f32[512]{0:T(512)S(1)}, f32[512]{0:T(512)S(1)}, f32[4]{0:T(128)S(1)}, f32[4]{0:T(128)S(1)}) all-reduce(f32[512]{0:T(512)S(1)} %get-tuple-element.184, f32[512]{0:T(512)S(1)} %get-tuple-element.183, f32[4]{0:T(128)S(1)} %get-tuple-element.186, f32[4]{0:T(128)S(1)} %get-tuple-element.185), channel_id=1, replica_groups=mesh['seq'=16,'tp'=8] {'tp'}, use_global_device_ids=true, to_apply=%region_3.0 | all-reduce | flops 1032 | bytes 8256 | tf_op jit(solution)/shard_map/psum | solution.py:85
  132.2 1.1 pad_maximum_fusion
  133.3 1.3 slice.118
  134.8 1.1 copy.24
  136.5 0.6 broadcast_and_fusion
  137.5 1.4 fusion.29
  139.1 1.3 fusion.27
  140.4 29.3 %all-gather.2 = f32[64,4,128]{2,1,0:T(4,128)S(1)} all-gather(f32[4,4,128]{2,1,0:T(4,128)S(1)} %bitcast.96), channel_id=4, replica_groups=mesh['seq'=16,'tp'=8] {'seq'}, dimensions={0}, use_global_device_ids=true | all-gather | bytes 139264 | tf_op jit(solution)/shard_map/all_gather | solution.py:14
  170.6 19.6 %all-gather.4 = f32[16,4,4]{2,1,0:T(4,128)S(1)} all-gather(f32[1,4,4]{2,1,0:T(4,128)S(1)} %bitcast.99), channel_id=3, replica_groups=mesh['seq'=16,'tp'=8] {'seq'}, dimensions={0}, use_global_device_ids=true | all-gather | bytes 1088 | tf_op jit(solution)/shard_map/all_gather | solution.py:14
  190.1 20.8 %all-gather.3 = f32[16,4,4]{2,1,0:T(4,128)S(1)} all-gather(f32[1,4,4]{2,1,0:T(4,128)S(1)} %bitcast.97), channel_id=2, replica_groups=mesh['seq'=16,'tp'=8] {'seq'}, dimensions={0}, use_global_device_ids=true | all-gather | bytes 1088 | tf_op jit(solution)/shard_map/all_gather | solution.py:14
  211.0 13.4 %fusion.3 = (f32[4,4,128]{2,1,0:T(4,128)S(1)}, f32[4,4,128,2048]{3,2,1,0:T(8,128)}) fusion(pred[4,128,2048]{2,1,0:T(8,128)(4,1)S(1)} %broadcast_and_fusion, bf16[4,2048,4,128]{3,1,2,0:T(8,128)(2,1)} %all-gather.11.cloned.1.call-done, bf16[4,128,4,64]{3,1,2,0:T(8,128)(2,1)S(1)} %copy.21, bf16[4,128,4,64]{3,1,2,0:T(8,128)(2,1)S(1)} %copy.20), kind=kOutput, calls=%fused_computation.10 | convolution fusion | flops 1087371264 | bytes 26746880 | tf_op jit(solution)/shard_map/sphe,snhe->shpn/dot_general | solution.py:39
  224.3 8.4 %fusion.4 = f32[4,4,128]{2,1,0:T(4,128)S(1)} fusion(f32[4,4,128,2048]{3,2,1,0:T(8,128)} %get-tuple-element.235, f32[4,4,128]{2,1,0:T(4,128)S(1)} %broadcast_maximum_fusion, pred[4,128,2048]{2,1,0:T(8,128)(4,1)S(1)} %broadcast_and_fusion), kind=kLoop, calls=%fused_computation.11 | loop fusion | flops 20969472 | bytes 17842176 | tf_op jit(solution)/shard_map/reduce_sum | solution.py:50
  232.7 51.6 %all-gather.13.cloned.1.call-done = bf16[4,2048,4,128]{3,1,2,0:T(8,128)(2,1)} async-done(((bf16[4,128,4,128]{3,1,2,0:T(8,128)(2,1)}), bf16[4,2048,4,128]{3,1,2,0:T(8,128)(2,1)}) %all-gather.13.cloned.1.call-update) | async-done | bytes 8388624 | tf_op jit(solution)/shard_map/all_gather | solution.py:128
  284.4 11.7 %divide_convert_fusion = bf16[4,128,4,128]{3,1,2,0:T(8,128)(2,1)S(1)} fusion(bf16[4,2048,4,128]{3,1,2,0:T(8,128)(2,1)} %all-gather.13.cloned.1.call-done, f32[4,4,128,2048]{3,2,1,0:T(8,128)} %get-tuple-element.235, f32[4,4,128]{2,1,0:T(4,128)S(1)} %broadcast_maximum_fusion, pred[4,128,2048]{2,1,0:T(8,128)(4,1)S(1)} %broadcast_and_fusion, ...), kind=kOutput, calls=%fused_computation.26 | convolution fusion | flops 1095237632 | bytes 26755072 | tf_op jit(solution)/shard_map/shpn,snhe->shpe/dot_general | solution.py:51
  296.1 0.4 copy.25
  296.5 4.3 convolution_convert_fusion
  300.9 1.6 while.19
  302.8 2.8 convolution_convert_fusion.1
  305.6 28.8 %psum.47 = bf16[4,4096]{1,0:T(4,128)(2,1)S(1)} all-reduce(bf16[4,4096]{1,0:T(4,128)(2,1)S(1)} %convolution_convert_fusion.1), channel_id=1, replica_groups=mesh['seq'=16,'tp'=8] {'tp'}, use_global_device_ids=true, to_apply=%region_16.17 | all-reduce | flops 16384 | bytes 65536 | tf_op jit(solution)/shard_map/psum | solution.py:169
  334.6 0.7 add_convert_fusion.3
  335.3 146.6 %all-reduce.3.cloned.1.call-done = bf16[512,4096]{1,0:T(8,128)(2,1)} async-done(((bf16[512,4096]{1,0:T(8,128)(2,1)}), bf16[512,4096]{1,0:T(8,128)(2,1)}) %all-reduce.3.cloned.1.call-update) | async-done | bytes 4194320 | tf_op jit(solution)/shard_map/psum | solution.py:168
  481.9 3.1 multiply_reduce_fusion
  484.9 3.3 convert_element_type.95
  488.2 1.0 add_convert_fusion
  (98 shorter events, 5.9 us)
Async XLA Ops:
  7.2 96.5 %all-gather.9.cloned.1.call-start = ((), (), s32[]{:S(2)}) async-start(), calls=%async_computation | async-start | bytes 4718592 | tf_op jit(solution)/shard_map/all_gather | solution.py:79
  7.9 203.1 %all-gather.11.cloned.1.call-start = ((), (), s32[]{:S(2)}) async-start(), calls=%async_computation.1 | async-start | bytes 8912896 | tf_op jit(solution)/shard_map/all_gather | solution.py:127
  38.4 92.3 %copy-start.5 = (f32[512]{0:T(512)S(1)}, f32[512]{0:T(512)}, u32[]{:S(2)}) copy-start(f32[512]{0:T(512)} %param.15) | copy-start | bytes 6148
  38.4 92.5 %copy-start.6 = (f32[512]{0:T(512)S(1)}, f32[512]{0:T(512)}, u32[]{:S(2)}) copy-start(f32[512]{0:T(512)} %param.14) | copy-start | bytes 6148
  114.3 1.7 copy-start.1
  116.4 19.6 %copy-start.7 = (s32[4]{0:T(128)S(1)}, s32[4]{0:T(128)}, u32[]{:S(2)}) copy-start(s32[4]{0:T(128)} %param.17) | copy-start | bytes 52
  133.3 151.1 %all-gather.13.cloned.1.call-start = ((), (), s32[]{:S(2)}) async-start(), calls=%async_computation.2 | async-start | bytes 8912896 | tf_op jit(solution)/shard_map/all_gather | solution.py:128
  135.9 346.0 %all-reduce.3.cloned.1.call-start = ((), (), s32[]{:S(2)}) async-start(), calls=%async_computation.3 | async-start | bytes 8388608 | tf_op jit(solution)/shard_map/psum | solution.py:168
  284.4 12.1 %copy-start = (bf16[512,4096]{1,0:T(8,128)(2,1)S(1)}, bf16[512,4096]{1,0:T(8,128)(2,1)}, u32[]{:S(2)}) copy-start(bf16[512,4096]{1,0:T(8,128)(2,1)} %param.13) | copy-start | bytes 12582916
  296.5 38.1 %copy-start.3 = (bf16[4,512]{1,0:T(4,128)(2,1)S(1)}, bf16[4,512]{1,0:T(4,128)(2,1)}, u32[]{:S(2)}) copy-start(bf16[4,512]{1,0:T(4,128)(2,1)} %param.11) | copy-start | bytes 12292
  296.5 38.1 %copy-start.4 = (f32[512]{0:T(512)S(1)}, f32[512]{0:T(512)}, u32[]{:S(2)}) copy-start(f32[512]{0:T(512)} %param.16) | copy-start | bytes 6148
  335.3 152.9 %copy-start.2 = (bf16[4,128,512]{2,1,0:T(8,128)(2,1)S(1)}, bf16[4,128,512]{2,1,0:T(8,128)(2,1)}, u32[]{:S(2)}) copy-start(bf16[4,128,512]{2,1,0:T(8,128)(2,1)} %param.10) | copy-start | bytes 1572868
Sparse Core Ops, SparseCore 0:
  9.6 93.9 all-gather.8
  133.4 77.0 all-gather.10
  213.6 70.7 all-gather.12
  301.0 180.8 all-reduce.2
where the time goes:
time: 496 us
  waiting for transfers between devices  264 us (53%)
  blocking collectives  136 us (27%)
  matrix products  51.9 us (10%)
  other arithmetic  23 us (5%)
  between operations  14.1 us (3%)
  local copies, waits for them, and re-layouts  6.25 us (1%)
    psum x1, waiting for transfers between devices, body(): lax.psum(part_rows.astype(jnp.bfloat16), 'tp').astype(jnp.float32)  147 us
    all_gather x3, blocking collectives, joined(): everything = jax.tree.map(lambda part: lax.all_gather(part, axis), value)  69.7 us
    all_gather x1, waiting for transfers between devices, body(): row_piece = lax.all_gather(flat_rows, 'tp', axis=1, tiled=True)  65.3 us
    all_gather x1, waiting for transfers between devices, body(): lax.all_gather(values, 'seq', axis=1, tiled=True)  51.6 us
    psum x1, blocking collectives, body(): lax.psum(part_new.astype(jnp.bfloat16), 'tp').astype(jnp.float32)  28.8 us
    all_gather x1, blocking collectives, body(): new_piece = lax.all_gather(new_tokens, 'tp', axis=1, tiled=True)  23.3 us
    psum x1, blocking collectives, body(): lax.psum((jnp.sum(query_rows * query_rows, -1), jnp.sum(key_rows * key_ro...  14.3 us
    dot_general x1, matrix products, fold_step(): jnp.einsum('sphe,snhe->shpn', queries, key_piece, preferred_element_type=...  13.4 us
  transfers between devices with their start and end apart: 4, of which 3 were waited for; matrix products, arithmetic and copies ran while one was open for 8% of the time, Pallas kernels for 0%

commit v1 on v0

--- a/solution.py
+++ b/solution.py
@@ -165,7 +165,7 @@
     part_rows = jnp.dot(attention, w_out, preferred_element_type=jnp.float32)
     part_new = jnp.dot(new_attention, w_out, preferred_element_type=jnp.float32)
     sum_rows, sum_new = (
-        lax.psum(part_rows.astype(jnp.bfloat16), "tp").astype(jnp.float32),
+        jnp.sum(lax.all_gather(part_rows.astype(jnp.bfloat16), "tp"), axis=0).astype(jnp.float32),
         lax.psum(part_new.astype(jnp.bfloat16), "tp").astype(jnp.float32),
     )
     mean_rows = jnp.mean(sum_rows * sum_rows, -1)

time: 496 us -> 968 us (1.95)
  waiting for transfers between devices: 264 us -> 732 us
  other arithmetic: 23 us -> 37.2 us
    all_gather x0 -> x1, waiting for transfers between devices: none -> 542 us  [body(): lax.all_gather(part_rows.astype(jnp.bfloat16), 'tp')]
    psum x1 -> x0, waiting for transfers between devices: 147 us -> none  [body(): lax.psum(part_rows.astype(jnp.bfloat16), 'tp').astype(jnp.float32)]
    all_gather x1, waiting for transfers between devices: 0.01 us -> 72 us  [body(): lax.all_gather(keys, 'seq', axis=1, tiled=True)]
    reduce_sum x0 -> x1, other arithmetic: none -> 14.2 us  [body(): jnp.sum(lax.all_gather(part_rows.astype(jnp.bfloat16), 'tp'), axis=0)]
  transfers between devices with their start and end apart: 4 -> 4, of which waited for: 3 -> 4; matrix products, arithmetic and copies ran while one was open for 8% -> 4% of each run, Pallas kernels for 0% -> 0%
where the time goes in v1:
time: 968 us
  waiting for transfers between devices  732 us (76%)
  blocking collectives  128 us (13%)
  matrix products  49.9 us (5%)
  other arithmetic  37.2 us (4%)
  between operations  14.1 us (1%)
    all_gather x1, waiting for transfers between devices, body(): lax.all_gather(part_rows.astype(jnp.bfloat16), 'tp')  542 us
    all_gather x1, waiting for transfers between devices, body(): lax.all_gather(keys, 'seq', axis=1, tiled=True)  72 us
    all_gather x1, waiting for transfers between devices, body(): row_piece = lax.all_gather(flat_rows, 'tp', axis=1, tiled=True)  65.3 us
    all_gather x3, blocking collectives, joined(): everything = jax.tree.map(lambda part: lax.all_gather(part, axis), value)  60.7 us
    all_gather x1, waiting for transfers between devices, body(): lax.all_gather(values, 'seq', axis=1, tiled=True)  52.2 us
    psum x1, blocking collectives, body(): lax.psum(part_new.astype(jnp.bfloat16), 'tp').astype(jnp.float32)  29.6 us
    all_gather x1, blocking collectives, body(): new_piece = lax.all_gather(new_tokens, 'tp', axis=1, tiled=True)  23.3 us
  transfers between devices with their start and end apart: 4, of which 4 were waited for; matrix products, arithmetic and copies ran while one was open for 4% of the time, Pallas kernels for 0%

profile of v1, /device:TPU:1, one launch (start us, length us, event | category | flops | bytes accessed | tf_op | source)
XLA Modules:
  0.0 968.1 jit_solution(16050541007025410287)
XLA Ops:
  7.2 0.7 all-gather.11.cloned.1.call-update
  7.9 23.3 %all_gather.41 = bf16[4,4096]{1,0:T(4,128)(2,1)S(1)} all-gather(bf16[4,512]{1,0:T(4,128)(2,1)} %param.11), channel_id=1, replica_groups=mesh['seq'=16,'tp'=8] {'tp'}, dimensions={1}, use_global_device_ids=true | all-gather | bytes 36864 | tf_op jit(solution)/shard_map/all_gather | solution.py:80
  31.3 6.3 convolution_bitcast_fusion
  37.8 0.5 multiply_cosine_fusion
  38.4 65.3 %all-gather.11.cloned.1.call-done = bf16[512,4096]{1,0:T(8,128)(2,1)} async-done(((bf16[512,512]{1,0:T(8,128)(2,1)}), bf16[512,4096]{1,0:T(8,128)(2,1)}) %all-gather.11.cloned.1.call-update) | async-done | bytes 4194320 | tf_op jit(solution)/shard_map/all_gather | solution.py:79
  103.7 10.6 %fusion.11 = f32[3,512,512]{1,2,0:T(8,128)S(1)} fusion(bf16[3,4096,512]{2,1,0:T(8,128)(2,1)} %param.12, bf16[512,4096]{1,0:T(8,128)(2,1)} %all-gather.11.cloned.1.call-done), kind=kOutput, calls=%fused_computation.21 | convolution fusion | flops 6442450944 | bytes 19922944 | tf_op jit(solution)/shard_map/tn,cnf->ctf/dot_general | solution.py:81
  114.3 1.7 copy-done.3
  116.0 0.4 multiply_reduce_fusion.2
  116.4 14.3 %all-reduce = (f32[512]{0:T(512)S(1)}, f32[512]{0:T(512)S(1)}, f32[4]{0:T(128)S(1)}, f32[4]{0:T(128)S(1)}) all-reduce(f32[512]{0:T(512)S(1)} %get-tuple-element.184, f32[512]{0:T(512)S(1)} %get-tuple-element.183, f32[4]{0:T(128)S(1)} %get-tuple-element.186, f32[4]{0:T(128)S(1)} %get-tuple-element.185), channel_id=1, replica_groups=mesh['seq'=16,'tp'=8] {'tp'}, use_global_device_ids=true, to_apply=%region_3.0 | all-reduce | flops 1032 | bytes 8256 | tf_op jit(solution)/shard_map/psum | solution.py:85
  132.2 1.1 pad_maximum_fusion
  133.3 1.3 slice.118
  134.8 1.1 copy.24
  136.5 0.6 broadcast_and_fusion
  137.9 72.0 %all-gather.13.cloned.1.call-done = bf16[4,2048,4,128]{3,1,2,0:T(8,128)(2,1)} async-done(((bf16[4,128,4,128]{3,1,2,0:T(8,128)(2,1)}), bf16[4,2048,4,128]{3,1,2,0:T(8,128)(2,1)}) %all-gather.13.cloned.1.call-update) | async-done | bytes 8388624 | tf_op jit(solution)/shard_map/all_gather | solution.py:127
  209.9 13.4 %fusion.3 = (f32[4,4,128]{2,1,0:T(4,128)S(1)}, f32[4,4,128,2048]{3,2,1,0:T(8,128)}) fusion(pred[4,128,2048]{2,1,0:T(8,128)(4,1)S(1)} %broadcast_and_fusion, bf16[4,2048,4,128]{3,1,2,0:T(8,128)(2,1)} %all-gather.13.cloned.1.call-done, bf16[4,128,4,64]{3,1,2,0:T(8,128)(2,1)S(1)} %copy.21, bf16[4,128,4,64]{3,1,2,0:T(8,128)(2,1)S(1)} %copy.20), kind=kOutput, calls=%fused_computation.10 | convolution fusion | flops 1087371264 | bytes 26746880 | tf_op jit(solution)/shard_map/sphe,snhe->shpn/dot_general | solution.py:39
  223.2 8.4 fusion.4
  231.6 52.2 %all-gather.15.cloned.1.call-done = bf16[4,2048,4,128]{3,1,2,0:T(8,128)(2,1)} async-done(((bf16[4,128,4,128]{3,1,2,0:T(8,128)(2,1)}), bf16[4,2048,4,128]{3,1,2,0:T(8,128)(2,1)}) %all-gather.15.cloned.1.call-update) | async-done | bytes 8388624 | tf_op jit(solution)/shard_map/all_gather | solution.py:128
  283.8 11.7 %divide_convert_fusion = bf16[4,128,4,128]{3,1,2,0:T(8,128)(2,1)S(1)} fusion(bf16[4,2048,4,128]{3,1,2,0:T(8,128)(2,1)} %all-gather.15.cloned.1.call-done, f32[4,4,128,2048]{3,2,1,0:T(8,128)} %get-tuple-element.235, f32[4,4,128]{2,1,0:T(4,128)S(1)} %broadcast_maximum_fusion, pred[4,128,2048]{2,1,0:T(8,128)(4,1)S(1)} %broadcast_and_fusion, ...), kind=kOutput, calls=%fused_computation.26 | convolution fusion | flops 1095237632 | bytes 26755072 | tf_op jit(solution)/shard_map/shpn,snhe->shpe/dot_general | solution.py:51
  295.6 0.4 copy.25
  296.0 4.4 convolution_convert_fusion
  301.9 20.6 %all-gather.3 = f32[64,4,128]{2,1,0:T(4,128)S(1)} all-gather(f32[4,4,128]{2,1,0:T(4,128)S(1)} %bitcast.98), channel_id=5, replica_groups=mesh['seq'=16,'tp'=8] {'seq'}, dimensions={0}, use_global_device_ids=true | all-gather | bytes 139264 | tf_op jit(solution)/shard_map/all_gather | solution.py:14
  322.6 20.3 %all-gather.4 = f32[16,4,4]{2,1,0:T(4,128)S(1)} all-gather(f32[1,4,4]{2,1,0:T(4,128)S(1)} %bitcast.99), channel_id=3, replica_groups=mesh['seq'=16,'tp'=8] {'seq'}, dimensions={0}, use_global_device_ids=true | all-gather | bytes 1088 | tf_op jit(solution)/shard_map/all_gather | solution.py:14
  342.8 19.8 %all-gather.5 = f32[16,4,4]{2,1,0:T(4,128)S(1)} all-gather(f32[1,4,4]{2,1,0:T(4,128)S(1)} %bitcast.101), channel_id=4, replica_groups=mesh['seq'=16,'tp'=8] {'seq'}, dimensions={0}, use_global_device_ids=true | all-gather | bytes 1088 | tf_op jit(solution)/shard_map/all_gather | solution.py:14
  362.8 1.6 while.19
  364.5 2.8 convolution_convert_fusion.1
  367.4 29.6 %psum.39 = bf16[4,4096]{1,0:T(4,128)(2,1)S(1)} all-reduce(bf16[4,4096]{1,0:T(4,128)(2,1)S(1)} %convolution_convert_fusion.1), channel_id=1, replica_groups=mesh['seq'=16,'tp'=8] {'tp'}, use_global_device_ids=true, to_apply=%region_16.17 | all-reduce | flops 16384 | bytes 65536 | tf_op jit(solution)/shard_map/psum | solution.py:169
  397.1 0.7 add_convert_fusion.3
  397.8 542.2 %all-gather.17.cloned.1.call-done = bf16[4096,4096]{1,0:T(8,128)(2,1)} async-done(((bf16[512,4096]{1,0:T(8,128)(2,1)}), bf16[4096,4096]{1,0:T(8,128)(2,1)}) %all-gather.17.cloned.1.call-update) | async-done | bytes 33554448 | tf_op jit(solution)/shard_map/all_gather | solution.py:168
  939.9 14.2 %reduce_sum.87 = bf16[512,4096]{1,0:T(8,128)(2,1)} reduce(bf16[8,512,4096]{2,1,0:T(8,128)(2,1)} %bitcast.89, bf16[]{:T(256)} %constant.82.clone.1), dimensions={0}, to_apply=%region_6.0 | reduce | flops 14680064 | bytes 37748736 | tf_op jit(solution)/shard_map/reduce_sum | solution.py:168
  954.1 3.1 multiply_reduce_fusion
  957.2 3.3 convert_element_type.97
  960.5 1.0 add_convert_fusion
  (103 shorter events, 6.7 us)
Async XLA Ops:
  7.2 96.5 %all-gather.11.cloned.1.call-start = ((), (), s32[]{:S(2)}) async-start(), calls=%async_computation | async-start | bytes 4718592 | tf_op jit(solution)/shard_map/all_gather | solution.py:79
  7.9 202.0 %all-gather.13.cloned.1.call-start = ((), (), s32[]{:S(2)}) async-start(), calls=%async_computation.1 | async-start | bytes 8912896 | tf_op jit(solution)/shard_map/all_gather | solution.py:127
  38.4 92.3 %copy-start.7 = (f32[512]{0:T(512)S(1)}, f32[512]{0:T(512)}, u32[]{:S(2)}) copy-start(f32[512]{0:T(512)} %param.15) | copy-start | bytes 6148
  38.4 92.5 %copy-start.8 = (f32[512]{0:T(512)S(1)}, f32[512]{0:T(512)}, u32[]{:S(2)}) copy-start(f32[512]{0:T(512)} %param.14) | copy-start | bytes 6148
  114.3 1.7 copy-start.3
  116.4 19.8 %copy-start.9 = (s32[4]{0:T(128)S(1)}, s32[4]{0:T(128)}, u32[]{:S(2)}) copy-start(s32[4]{0:T(128)} %param.17) | copy-start | bytes 52
  133.3 150.5 %all-gather.15.cloned.1.call-start = ((), (), s32[]{:S(2)}) async-start(), calls=%async_computation.2 | async-start | bytes 8912896 | tf_op jit(solution)/shard_map/all_gather | solution.py:128
  135.9 804.0 %all-gather.17.cloned.1.call-start = ((), (), s32[]{:S(2)}) async-start(), calls=%async_computation.3 | async-start | bytes 37748736 | tf_op jit(solution)/shard_map/all_gather | solution.py:168
  283.8 12.1 %copy-start.2 = (bf16[512,4096]{1,0:T(8,128)(2,1)S(1)}, bf16[512,4096]{1,0:T(8,128)(2,1)}, u32[]{:S(2)}) copy-start(bf16[512,4096]{1,0:T(8,128)(2,1)} %param.13) | copy-start | bytes 12582916
  296.0 5.1 copy-start
  296.0 5.7 copy-start.1
  296.0 101.1 %copy-start.5 = (bf16[4,512]{1,0:T(4,128)(2,1)S(1)}, bf16[4,512]{1,0:T(4,128)(2,1)}, u32[]{:S(2)}) copy-start(bf16[4,512]{1,0:T(4,128)(2,1)} %param.11) | copy-start | bytes 12292
  296.0 101.1 %copy-start.6 = (f32[512]{0:T(512)S(1)}, f32[512]{0:T(512)}, u32[]{:S(2)}) copy-start(f32[512]{0:T(512)} %param.16) | copy-start | bytes 6148
  954.1 6.4 copy-start.4
Sparse Core Ops, SparseCore 0:
  9.6 93.9 all-gather.10
  133.4 76.3 all-gather.12
  213.0 70.8 all-gather.14
  300.6 639.2 all-gather.16
